TPU v7x, 128 devices: a whole 4x4x4 slice. The times are simulated.
128 devices in a mesh: req: 8 (over y, x_hi), row: 4 (over x_lo, core), col: 4 (over z).
Axes of the slice: x: 4 (x_hi: 2, x_lo: 2; x = x_hi * 2 + x_lo), y: 4, z: 4, core: 2. Of those that a mesh axis runs over, the one named last changes fastest.
Arguments:
- text_embed: bfloat16 [6144, 4096], P(('req', 'col'), 'row')
- vis_embed: bfloat16 [4096, 4096], P(('req', 'col'), 'row')
- vis_segment: int32 [4096], P(('req', 'col')), may hold values from 0 to 20, never falling along the last dimension, each value on 1 to 256 neighbouring positions
- vis_valid: int32 [4096], P(('req', 'col')), may hold values 0 or 1
- vis_gain: bfloat16 [4096], P('row'), may hold values from 0.25 to 1.75
- vis_wq: bfloat16 [4096, 4096], P('row', 'col')
- vis_wk: bfloat16 [4096, 4096], P('row', 'col')
- vis_wv: bfloat16 [4096, 4096], P('row', 'col'), may hold values from -0.09375 to 0.09375
- vis_wo: bfloat16 [4096, 4096], P('col', 'row'), may hold values from -0.09375 to 0.09375
- dec_gain: bfloat16 [4096], P('row'), may hold values from 0.25 to 1.75
- dec_wq: bfloat16 [4096, 4096], P('row', 'col')
- dec_wk: bfloat16 [4096, 4096], P('row', 'col')
- dec_wv: bfloat16 [4096, 4096], P('row', 'col'), may hold values from -0.09375 to 0.09375
- dec_wo: bfloat16 [4096, 4096], P('col', 'row'), may hold values from -0.09375 to 0.09375
Outputs:
- hidden_out: bfloat16 [6144, 4096], P(('req', 'col'), 'row')
Inputs may be any that keep to these rules, and one draw needn't show every extreme that they name: `vis_segment`: images take consecutive slots in order, each 1 to 256 slots, one exactly 256.
All inputs are finite; a program needn't handle non-finite values. No bound on the sum of `vis_valid` on one device may be relied on, other than what follows from the above.
Results may differ from a plain program's by a relative error of at most 0.008.
Values may be sent and summed in bfloat16 or wider, within the bound.
No kernel may reach another device: no remote copies, remote signals or barrier semaphores. Data moves between devices by JAX's collectives and lax.ppermute only.
A program may use at most 192 MiB of HBM per device.

v0:
```python
import jax
import jax.numpy as jnp
from jax import lax
from jax.sharding import PartitionSpec as P

D = 4096
HD = 128
MAXIMG = 256


def with_halo(cells, sides, width):
    for axis, dim in sides:
        count = lax.axis_size(axis)
        ends = count - 1
        head = lax.slice_in_dim(cells, 0, width, axis=dim)
        tail = lax.slice_in_dim(cells, cells.shape[dim] - width, cells.shape[dim], axis=dim)
        cells = jnp.concatenate(
            [
                lax.ppermute(tail, axis, [(i, (i + 1) % count) for i in range(ends)]),
                cells,
                lax.ppermute(head, axis, [((i + 1) % count, i) for i in range(ends)]),
            ],
            axis=dim,
        )
    return cells


def passed_along(shard, axis, by):
    size = lax.axis_size(axis)
    pairs = [(i, i + by) for i in range(size) if 0 <= i + by < size]
    return lax.ppermute(shard, axis, pairs)


def norm_local(values, gain):
    floats = values.astype(jnp.float32)
    squares = jnp.sum(floats * floats, axis=-1)
    totals = lax.psum(squares, "row")
    factor = lax.rsqrt(totals / D + 1e-05)
    return (floats * factor[:, None] * gain.astype(jnp.float32)[None, :]).astype(jnp.bfloat16)


def gather_cols(values):
    return lax.all_gather(values, "col", axis=0, tiled=True)


def out_project(attended, weight):
    whole = lax.all_gather(attended, "row", axis=0, tiled=True)
    return lax.psum_scatter(
        jnp.dot(whole, weight, preferred_element_type=jnp.float32).astype(jnp.bfloat16),
        "col",
        scatter_dimension=0,
        tiled=True,
    ).astype(jnp.float32)


def split_heads(values):
    return values.reshape(values.shape[0], values.shape[1] // HD, HD)


def attend_block(queries, keys, values, allowed):
    query_heads = split_heads(queries)
    scores = jnp.einsum(
        "qhd,khd->hqk", query_heads, split_heads(keys), preferred_element_type=jnp.float32
    ) * HD ** (-0.5)
    scores = jnp.where(allowed[None], scores, -1e30)
    peak = jnp.max(scores, axis=-1, keepdims=True)
    weights = jnp.where(allowed[None], jnp.exp(scores - peak), 0.0)
    mass = jnp.sum(weights, axis=-1)
    summed = jnp.einsum(
        "hqk,khd->qhd",
        weights.astype(jnp.bfloat16),
        split_heads(values),
        preferred_element_type=jnp.float32,
    )
    result = summed / jnp.transpose(mass)[:, :, None]
    return result.reshape(queries.shape[0], queries.shape[1]).astype(jnp.bfloat16)


def fold_step(carry, query_heads, query_slots, key_heads, value_heads):
    peak, mass, accum = carry
    piece_slots = jnp.arange(key_heads.shape[0], dtype=jnp.int32)
    allowed = query_slots[:, None] >= piece_slots[None, :]
    scores = jnp.einsum(
        "qhd,khd->hqk", query_heads, key_heads, preferred_element_type=jnp.float32
    ) * HD ** (-0.5)
    scores = jnp.where(allowed[None], scores, -1e30)
    new_peak = jnp.maximum(peak, jnp.max(scores, axis=-1))
    weights = jnp.where(allowed[None], jnp.exp(scores - new_peak[:, :, None]), 0.0)
    summed = jnp.einsum(
        "hqk,khd->hqd",
        weights.astype(jnp.bfloat16),
        value_heads,
        preferred_element_type=jnp.float32,
    )
    return (new_peak, jnp.sum(weights, axis=-1), summed)


def start_state(head_count, query_count):
    return (
        jnp.full((head_count, query_count), -1e30, jnp.float32),
        jnp.zeros((head_count, query_count), jnp.float32),
        jnp.zeros((head_count, query_count, HD), jnp.float32),
    )


def head_project(values, weights):
    count = values.shape[0]
    row_count = lax.axis_size("row")
    width = weights[0].shape[1]
    parts = [
        jnp.dot(values, w, preferred_element_type=jnp.float32)
        .astype(jnp.bfloat16)
        .reshape(count, row_count, width // row_count)
        for w in weights
    ]
    stacked = jnp.stack(parts, axis=2).transpose(1, 0, 2, 3)
    stacked = stacked.reshape(row_count * count, len(weights) * (width // row_count))
    return lax.psum_scatter(stacked, "row", scatter_dimension=0, tiled=True)


def out_project_heads(attended, weight):
    row_count = lax.axis_size("row")
    whole = lax.all_gather(attended, "row", axis=0, tiled=False)
    shaped = weight.reshape(row_count, weight.shape[0] // row_count, weight.shape[1])
    summed = jnp.einsum("rtf,rfo->to", whole, shaped, preferred_element_type=jnp.float32)
    return lax.psum_scatter(
        summed.astype(jnp.bfloat16), "col", scatter_dimension=0, tiled=True
    ).astype(jnp.float32)


def per_device(
    text_embed,
    vis_embed,
    vis_segment,
    vis_valid,
    vis_gain,
    vis_wq,
    vis_wk,
    vis_wv,
    vis_wo,
    dec_gain,
    dec_wq,
    dec_wk,
    dec_wv,
    dec_wo,
):
    row_count = lax.axis_size("row")
    col_count = lax.axis_size("col")
    width = vis_wq.shape[1]
    local = width // row_count
    margin = MAXIMG - 1
    piece_ids = lax.all_gather(jnp.stack([vis_segment, vis_valid]), "col", axis=1, tiled=True)
    piece_len = piece_ids.shape[1]
    framed_ids = with_halo(piece_ids, (("req", 1),), margin)
    total_slots = piece_len * lax.axis_size("req")
    prompt_rows = text_embed.shape[0]
    prompt_total = prompt_rows * lax.axis_size("req") * col_count
    window_len = piece_len + 2 * margin
    window_start = lax.axis_index("req") * piece_len - margin
    window_index = jnp.arange(window_len, dtype=jnp.int32)
    key_slots = window_start + window_index
    inside = (key_slots >= 0) & (key_slots < total_slots)
    key_segment = framed_ids[0]
    key_valid = framed_ids[1]
    begins = jnp.concatenate([jnp.ones((1,), jnp.bool_), key_segment[1:] != key_segment[:-1]])
    begins = begins | (key_slots == 0)
    image_first = lax.cummax(jnp.where(begins, key_slots, window_start), axis=0)
    target_window = image_first * prompt_total // total_slots + key_slots - image_first
    vis_cols = gather_cols(norm_local(vis_embed, vis_gain))
    vis_proj = head_project(vis_cols, (vis_wq, vis_wk, vis_wv))
    vis_pairs = jnp.stack([vis_proj[:, local : 2 * local], vis_proj[:, 2 * local :]])
    framed = with_halo(vis_pairs, (("req", 1),), margin)
    query_local = margin + jnp.arange(piece_len, dtype=jnp.int32)
    query_slots = window_start + query_local
    query_segment = key_segment[query_local]
    seen = (
        inside[None, :]
        & (query_segment[:, None] == key_segment[None, :])
        & ((key_valid[None, :] == 1) | (query_slots[:, None] == key_slots[None, :]))
    )
    vis_att = attend_block(vis_proj[:, :local], framed[0], framed[1], seen)
    vis_out = (vis_embed.astype(jnp.float32) + out_project_heads(vis_att, vis_wo)).astype(
        jnp.bfloat16
    )
    device_place = lax.axis_index("req") * col_count + lax.axis_index("col")
    owned = device_place * prompt_rows + jnp.arange(prompt_rows, dtype=jnp.int32)
    slot_rows = vis_out.shape[0]
    following = passed_along(vis_out, ("req", "col"), -1)
    near_rows = jnp.concatenate([vis_out, following], axis=0)
    near_local = (
        margin + lax.axis_index("col") * slot_rows + jnp.arange(2 * slot_rows, dtype=jnp.int32)
    )
    near_slots = window_start + near_local
    present = near_slots < total_slots
    near_target = jnp.where(present, target_window[near_local], -1)
    near_valid = key_valid[near_local]
    onehot = ((owned[:, None] == near_target[None, :]) & (near_valid[None, :] == 1)).astype(
        jnp.bfloat16
    )
    carried = jnp.dot(onehot, near_rows, preferred_element_type=jnp.float32)
    mixed = (text_embed.astype(jnp.float32) + carried).astype(jnp.bfloat16)
    dec_cols = gather_cols(norm_local(mixed, dec_gain))
    dec_proj = head_project(dec_cols, (dec_wq, dec_wk, dec_wv))
    dec_rows = dec_cols.shape[0]
    dec_pairs = jnp.stack([dec_proj[:, local : 2 * local], dec_proj[:, 2 * local :]])
    piece = lax.all_gather(dec_pairs, "req", axis=1, tiled=True)
    token_slots = lax.axis_index("req") * dec_rows + jnp.arange(dec_rows, dtype=jnp.int32)
    all_slots = jnp.arange(piece.shape[1], dtype=jnp.int32)
    causal = token_slots[:, None] >= all_slots[None, :]
    dec_att = attend_block(dec_proj[:, :local], piece[0], piece[1], causal)
    return (mixed.astype(jnp.float32) + out_project_heads(dec_att, dec_wo)).astype(jnp.bfloat16)


def solution(mesh):
    return jax.shard_map(
        per_device,
        mesh=mesh,
        in_specs=(
            P(("req", "col"), "row"),
            P(("req", "col"), "row"),
            P(("req", "col")),
            P(("req", "col")),
            P("row"),
            P("row", "col"),
            P("row", "col"),
            P("row", "col"),
            P("col", "row"),
            P("row"),
            P("row", "col"),
            P("row", "col"),
            P("row", "col"),
            P("col", "row"),
        ),
        out_specs=P(("req", "col"), "row"),
        check_vma=False,
    )
```

profile of v0, /device:TPU:0, one launch (start us, length us, event | category | flops | bytes accessed | tf_op | source)
XLA Modules:
  0.0 563.6 jit_solution(1932380565323348486)
XLA Ops:
  6.5 1.2 fusion.34
  7.8 7.0 %psum.14 = f32[128]{0:T(128)S(1)} all-reduce(f32[128]{0:T(128)S(1)} %fusion.34), channel_id=1, replica_groups=mesh['req'=8,'row'=4,'col'=4] {'row'}, use_global_device_ids=true, to_apply=%region_3.4 | all-reduce | flops 128 | bytes 1024 | tf_op jit(solution)/shard_map/psum | solution.py:37
  15.4 1.8 fusion.36
  17.3 26.4 %all-gather.6.cloned.1.call-done = bf16[512,1024]{1,0:T(8,128)(2,1)} async-done(((bf16[128,1024]{1,0:T(8,128)(2,1)}), bf16[512,1024]{1,0:T(8,128)(2,1)}) %all-gather.6.cloned.1.call-update) | async-done | bytes 1048592 | tf_op jit(solution)/shard_map/all_gather | solution.py:43
  43.7 4.2 convolution_convert_fusion.3
  47.9 1.9 stack_reshape.20
  49.7 2.4 copy.31
  52.1 4.2 convolution_convert_fusion.5
  56.3 1.9 stack_reshape.18
  58.1 2.4 copy.29
  60.5 4.2 convolution_convert_fusion.4
  64.7 1.9 stack_reshape.19
  66.5 2.3 copy.30
  68.8 4.2 pad_maximum_fusion.1
  73.0 2.7 copy.45
  76.4 8.6 %all_gather.20 = s32[2,512]{1,0:T(2,128)S(1)} all-gather(s32[2,128]{1,0:T(2,128)S(1)} %pad_add_fusion.1), channel_id=1, replica_groups=mesh['req'=8,'row'=4,'col'=4] {'col'}, dimensions={1}, use_global_device_ids=true | all-gather | bytes 5120 | tf_op jit(solution)/shard_map/all_gather | solution.py:152
  85.0 4.9 collective-permute-start
  89.9 1.3 collective-permute-start.1
  91.3 5.6 collective-permute-done.1
  97.0 16.1 %reduce-scatter.5.cloned.1.call-done = bf16[512,768]{0,1:T(8,128)(2,1)} async-done(((bf16[2048,768]{0,1:T(8,128)(2,1)}), bf16[512,768]{0,1:T(8,128)(2,1)}) %reduce-scatter.5.cloned.1.call-update) | async-done | bytes 786448 | tf_op jit(solution)/shard_map/reduce_scatter | solution.py:118
  113.1 1.2 fusion.67
  115.1 5.3 collective-permute-start.2
  120.5 1.7 collective-permute-start.3
  122.2 2.3 gather_fusion.2
  125.9 7.8 %collective-permute-done.3 = bf16[2,255,256]{1,2,0:T(8,128)(2,1)} collective-permute-done((bf16[2,255,256]{1,2,0:T(8,128)(2,1)}, bf16[2,255,256]{1,2,0:T(8,128)(2,1)}, u32[]{:S(2)}, u32[]{:S(2)}) %collective-permute-start.3) | collective-permute-done | bytes 261152 | tf_op jit(solution)/shard_map/ppermute | solution.py:21
  133.7 1.5 pad_maximum_fusion.2
  136.1 4.6 fusion.70
  140.7 2.4 fusion.25
  144.0 21.4 %all-gather.8.cloned.1.call-done = bf16[4,512,256]{2,1,0:T(8,128)(2,1)} async-done(((bf16[1,512,256]{2,1,0:T(8,128)(2,1)}), bf16[4,512,256]{2,1,0:T(8,128)(2,1)}) %all-gather.8.cloned.1.call-update) | async-done | bytes 1048592 | tf_op jit(solution)/shard_map/all_gather | solution.py:123
  165.5 4.2 bitcast_convert_fusion.1
  170.4 1.4 gather_fusion.1
  171.9 22.6 %reduce-scatter.7.cloned.1.call-done = bf16[128,1024]{1,0:T(8,128)(2,1)} async-done(((bf16[512,1024]{1,0:T(8,128)(2,1)}), bf16[128,1024]{1,0:T(8,128)(2,1)}) %reduce-scatter.7.cloned.1.call-update) | async-done | bytes 262160 | tf_op jit(solution)/shard_map/reduce_scatter | solution.py:126
  194.5 1.0 fusion.37
  195.5 1.3 collective-permute-start.4
  196.9 1.4 gather_fusion
  198.2 5.6 collective-permute-done.4
  203.8 1.4 multiply_reduce_fusion
  205.2 5.7 %psum.15 = f32[192]{0:T(256)S(1)} all-reduce(f32[192]{0:T(256)S(1)} %get-tuple-element.23), channel_id=1, replica_groups=mesh['req'=8,'row'=4,'col'=4] {'row'}, use_global_device_ids=true, to_apply=%region_9.10 | all-reduce | flops 192 | bytes 1536 | tf_op jit(solution)/shard_map/psum | solution.py:37
  212.0 30.4 %all-gather.10.cloned.1.call-done = bf16[768,1024]{1,0:T(8,128)(2,1)} async-done(((bf16[192,1024]{1,0:T(8,128)(2,1)}), bf16[768,1024]{1,0:T(8,128)(2,1)}) %all-gather.10.cloned.1.call-update) | async-done | bytes 1572880 | tf_op jit(solution)/shard_map/all_gather | solution.py:43
  242.5 5.0 convolution_convert_fusion
  247.5 3.9 stack_reshape.23
  251.3 4.2 copy.37
  255.6 5.0 convolution_convert_fusion.2
  260.6 3.9 stack_reshape.21
  264.5 4.2 copy.35
  268.7 5.0 convolution_convert_fusion.1
  273.7 3.8 stack_reshape.22
  277.6 4.2 copy.36
  281.8 6.0 %pad_maximum_fusion = bf16[768,4,3,256]{0,1,3,2:T(4,128)(2,1)S(1)} fusion(bf16[768,4,1,256]{0,1,3,2:T(4,128)(2,1)} %copy.37, bf16[768,4,1,256]{0,1,3,2:T(4,128)(2,1)} %copy.36, bf16[768,4,1,256]{0,1,3,2:T(4,128)(2,1)} %copy.35), kind=kLoop, calls=%fused_computation.14 | loop fusion | flops 4718592 | bytes 9437184 | tf_op jit(solution)/shard_map/stack | solution.py:116
  287.8 3.2 copy.46
  291.0 49.6 %reduce-scatter.9.cloned.1.call-done = bf16[768,768]{0,1:T(8,128)(2,1)} async-done(((bf16[3072,768]{0,1:T(8,128)(2,1)}), bf16[768,768]{0,1:T(8,128)(2,1)}) %reduce-scatter.9.cloned.1.call-update) | async-done | bytes 1179664 | tf_op jit(solution)/shard_map/reduce_scatter | solution.py:118
  340.7 1.3 fusion.65
  342.0 1.0 pad_maximum_fusion.3
  343.2 5.7 %iota_compare_fusion = pred[768,6144]{1,0:T(8,128)(4,1)} fusion(s32[768]{0:T(1024)S(1)} %iota_add_fusion), kind=kLoop, calls=%fused_computation.12 | loop fusion | flops 4718592 | bytes 4721664 | tf_op jit(solution)/shard_map/ge | solution.py:209
  348.9 83.6 %all-gather.12.cloned.1.call-done = bf16[2,6144,256]{1,2,0:T(8,128)(2,1)} async-done(((bf16[2,768,256]{1,2,0:T(8,128)(2,1)}), bf16[2,6144,256]{1,2,0:T(8,128)(2,1)}) %all-gather.12.cloned.1.call-update) | async-done | bytes 6291472 | tf_op jit(solution)/shard_map/all_gather | solution.py:206
  432.5 5.4 fusion.64
  437.9 14.7 %fusion.72 = f32[2,768,6144]{2,1,0:T(8,128)} fusion(bf16[768,2,128]{0,2,1:T(8,128)(2,1)S(1)} %bitcast.96, bf16[6144,2,128]{0,2,1:T(8,128)(2,1)S(1)} %bitcast.90), kind=kOutput, calls=%fused_computation.120 | convolution fusion | flops 2415919104 | bytes 41287680 | tf_op jit(solution)/shard_map/qhd,khd->hqk/dot_general | solution.py:62
  452.7 36.8 %fusion.71 = (f32[2,768]{1,0:T(2,128)S(1)}, bf16[2,768,6144]{2,1,0:T(8,128)(2,1)}) fusion(f32[2,768,6144]{2,1,0:T(8,128)} %fusion.72, pred[768,6144]{1,0:T(8,128)(4,1)S(1)} %bitcast.94), kind=kOutput, calls=%fused_computation.119 | output fusion | flops 75503616 | bytes 61347840 | tf_op jit(solution)/shard_map/sub | solution.py:67
  489.5 10.4 %fusion.31 = bf16[768,2,128]{0,2,1:T(8,128)(2,1)S(1)} fusion(bf16[6144,2,128]{0,2,1:T(8,128)(2,1)} %bitcast.95, bf16[2,768,6144]{2,1,0:T(8,128)(2,1)} %get-tuple-element.26, f32[768,2]{0,1:T(2,128)S(1)} %bitcast.107), kind=kOutput, calls=%fused_computation.41 | convolution fusion | flops 2416312320 | bytes 22419456 | tf_op jit(solution)/shard_map/hqk,khd->qhd/dot_general | solution.py:69
  499.9 0.9 copy.40
  500.9 22.7 %all-gather.14.cloned.1.call-done = bf16[4,768,256]{2,1,0:T(8,128)(2,1)} async-done(((bf16[1,768,256]{2,1,0:T(8,128)(2,1)}), bf16[4,768,256]{2,1,0:T(8,128)(2,1)}) %all-gather.14.cloned.1.call-update) | async-done | bytes 1572880 | tf_op jit(solution)/shard_map/all_gather | solution.py:123
  523.6 4.4 bitcast_convert_fusion
  528.0 27.0 %reduce-scatter.11.cloned.1.call-done = bf16[192,1024]{1,0:T(8,128)(2,1)} async-done(((bf16[768,1024]{1,0:T(8,128)(2,1)}), bf16[192,1024]{1,0:T(8,128)(2,1)}) %reduce-scatter.11.cloned.1.call-update) | async-done | bytes 393232 | tf_op jit(solution)/shard_map/reduce_scatter | solution.py:126
  555.0 1.8 add_convert_fusion
  (69 shorter events, 8.0 us)
Async XLA Ops:
  6.5 517.1 %copy-start = (bf16[1024,1024]{1,0:T(8,128)(2,1)S(1)}, bf16[1024,1024]{1,0:T(8,128)(2,1)}, u32[]{:S(2)}) copy-start(bf16[1024,1024]{1,0:T(8,128)(2,1)} %param.27) | copy-start | bytes 6291460
  6.5 37.1 %all-gather.6.cloned.1.call-start = ((), (), s32[]{:S(2)}) async-start(), calls=%async_computation.4 | async-start | bytes 1310720 | tf_op jit(solution)/shard_map/all_gather | solution.py:43
  17.2 95.9 %reduce-scatter.5.cloned.1.call-start = ((), (), s32[]{:S(2)}) async-start(), calls=%async_computation.5 | async-start | bytes 3932160 | tf_op jit(solution)/shard_map/reduce_scatter | solution.py:118
  75.7 0.7 copy-start.3
  75.7 0.7 copy-start.4
  75.7 89.7 %all-gather.8.cloned.1.call-start = ((), (), s32[]{:S(2)}) async-start(), calls=%async_computation.6 | async-start | bytes 1310720 | tf_op jit(solution)/shard_map/all_gather | solution.py:123
  85.0 6.3 %collective-permute-start = (s32[2,255]{1,0:T(2,128)S(1)}, s32[2,255]{1,0:T(2,128)S(1)}, u32[]{:S(2)}, u32[]{:S(2)}) collective-permute-start(s32[2,255]{1,0:T(2,128)S(1)} %get-tuple-element.19), channel_id=1, source_target_pairs={{0,16},{16,32},{32,48},{48,64},{64,80},{80,96},{96,112},{1,17},{17... | collective-permute-start | bytes 6128 | tf_op jit(solution)/shard_map/ppermute | solution.py:19
  89.9 7.0 %collective-permute-start.1 = (s32[2,255]{1,0:T(2,128)S(1)}, s32[2,255]{1,0:T(2,128)S(1)}, u32[]{:S(2)}, u32[]{:S(2)}) collective-permute-start(s32[2,255]{1,0:T(2,128)S(1)} %get-tuple-element.20), channel_id=1, source_target_pairs={{16,0},{32,16},{48,32},{64,48},{80,64},{96,80},{112,96},{17,1},{33... | collective-permute-start | bytes 6128 | tf_op jit(solution)/shard_map/ppermute | solution.py:21
  115.1 10.8 %collective-permute-start.2 = (bf16[2,255,256]{1,2,0:T(8,128)(2,1)}, bf16[2,255,256]{1,2,0:T(8,128)(2,1)}, u32[]{:S(2)}, u32[]{:S(2)}) collective-permute-start(bf16[2,255,256]{1,2,0:T(8,128)(2,1)} %get-tuple-element.15), channel_id=1, source_target_pairs={{0,16},{16,32},{32,48},{48,64},{64,80},{80,96},{96,112},{1,17},{17... | collective-permute-start | bytes 783368 | tf_op jit(solution)/shard_map/ppermute | solution.py:19
  120.5 13.3 %collective-permute-start.3 = (bf16[2,255,256]{1,2,0:T(8,128)(2,1)}, bf16[2,255,256]{1,2,0:T(8,128)(2,1)}, u32[]{:S(2)}, u32[]{:S(2)}) collective-permute-start(bf16[2,255,256]{1,2,0:T(8,128)(2,1)} %get-tuple-element.16), channel_id=1, source_target_pairs={{16,0},{32,16},{48,32},{64,48},{80,64},{96,80},{112,96},{17,1},{33... | collective-permute-start | bytes 783368 | tf_op jit(solution)/shard_map/ppermute | solution.py:21
  144.0 50.5 %reduce-scatter.7.cloned.1.call-start = ((), (), s32[]{:S(2)}) async-start(), calls=%async_computation.7 | async-start | bytes 1310720 | tf_op jit(solution)/shard_map/reduce_scatter | solution.py:126
  165.5 4.3 copy-start.2
  169.6 24.9 %copy-start.1 = (bf16[128,1024]{1,0:T(8,128)(2,1)S(1)}, bf16[128,1024]{1,0:T(8,128)(2,1)}, u32[]{:S(2)}) copy-start(bf16[128,1024]{1,0:T(8,128)(2,1)} %param.15) | copy-start | bytes 786436
  169.7 72.8 %all-gather.10.cloned.1.call-start = ((), (), s32[]{:S(2)}) async-start(), calls=%async_computation.8 | async-start | bytes 1966080 | tf_op jit(solution)/shard_map/all_gather | solution.py:43
  195.5 8.3 %collective-permute-start.4 = (bf16[128,1024]{1,0:T(8,128)(2,1)S(1)}, bf16[128,1024]{1,0:T(8,128)(2,1)S(1)}, u32[]{:S(2)}, u32[]{:S(2)}) collective-permute-start(bf16[128,1024]{1,0:T(8,128)(2,1)S(1)} %fusion.37), channel_id=1, source_target_pairs={{1,0},{2,1},{3,2},{16,3},{17,16},{18,17},{19,18},{32,19},{33,32},{... | collective-permute-start | bytes 786440 | tf_op jit(solution)/shard_map/ppermute | solution.py:31
  211.8 128.8 %reduce-scatter.9.cloned.1.call-start = ((), (), s32[]{:S(2)}) async-start(), calls=%async_computation.9 | async-start | bytes 5898240 | tf_op jit(solution)/shard_map/reduce_scatter | solution.py:118
  291.0 141.6 %all-gather.12.cloned.1.call-start = ((), (), s32[]{:S(2)}) async-start(), calls=%async_computation.10 | async-start | bytes 7077888 | tf_op jit(solution)/shard_map/all_gather | solution.py:206
  342.9 180.7 %all-gather.14.cloned.1.call-start = ((), (), s32[]{:S(2)}) async-start(), calls=%async_computation.11 | async-start | bytes 1966080 | tf_op jit(solution)/shard_map/all_gather | solution.py:123
  432.5 20.1 %slice-start = ((s8[4718592]{0:T(1024)(128)(4,1)}), s8[4194304]{0:T(1024)(128)(4,1)S(1)}, s32[]{:S(2)}) async-start(s8[4718592]{0:T(1024)(128)(4,1)} %bitcast.93), calls=%async_computation.13 | async-start | bytes 8388608
  437.9 14.7 %slice-start.1 = ((s8[4718592]{0:T(1024)(128)(4,1)}), s8[524288]{0:T(1024)(128)(4,1)S(1)}, s32[]{:S(2)}) async-start(s8[4718592]{0:T(1024)(128)(4,1)} %bitcast.93), calls=%async_computation.14 | async-start | bytes 1048576
  500.9 54.2 %reduce-scatter.11.cloned.1.call-start = ((), (), s32[]{:S(2)}) async-start(), calls=%async_computation.12 | async-start | bytes 1966080 | tf_op jit(solution)/shard_map/reduce_scatter | solution.py:126
Sparse Core Ops, SparseCore 0:
  17.4 26.2 all-gather.5
  75.9 37.1 reduce-scatter.4
  144.1 21.2 all-gather.7
  169.8 24.6 reduce-scatter.6
  211.9 30.5 all-gather.9
  291.1 49.5 reduce-scatter.8
  343.3 89.2 all-gather.11
  501.0 22.6 all-gather.13
  528.1 26.8 reduce-scatter.10
where the time goes:
time: 571 us; the launch traced here: 564 us
  waiting for transfers between devices  320 us (56%)
  matrix products  69.7 us (12%)
  other arithmetic  64.9 us (11%)
  local copies, waits for them, and re-layouts  59.1 us (10%)
  blocking collectives  21.2 us (4%)
  starting transfers between devices  15.2 us (3%)
  between operations  13.7 us (2%)
    all_gather x1, waiting for transfers between devices, per_device(): piece = lax.all_gather(dec_pairs, 'req', axis=1, tiled=True)  83.6 us
    reduce_scatter x2, waiting for transfers between devices, head_project(): return lax.psum_scatter(stacked, 'row', scatter_dimension=0, tiled=True)  65.7 us
    all_gather x2, waiting for transfers between devices, gather_cols(): return lax.all_gather(values, 'col', axis=0, tiled=True)  56.8 us
    reduce_scatter x2, waiting for transfers between devices, out_project_heads(): lax.psum_scatter(summed.astype(jnp.bfloat16), 'col', scatter_dimension=0,...  49.6 us
    all_gather x2, waiting for transfers between devices, out_project_heads(): whole = lax.all_gather(attended, 'row', axis=0, tiled=False)  44.1 us
    another operation x12, local copies, waits for them, and re-layouts, head_project(): stacked = jnp.stack(parts, axis=2).transpose(1, 0, 2, 3)  36.9 us
    sub x1, other arithmetic, attend_block(): weights = jnp.where(allowed[None], jnp.exp(scores - peak), 0.0)  36.8 us
    dot_general x6, matrix products, head_project(): jnp.dot(values, w, preferred_element_type=jnp.float32).astype(jnp.bfloat16)  27.6 us
  transfers between devices with their start and end apart: 14, of which 13 were waited for; matrix products, arithmetic and copies ran while one was open for 2% of the time, Pallas kernels for 0%

commit v1 on v0

--- a/solution.py
+++ b/solution.py
@@ -6,6 +6,12 @@
 D = 4096
 HD = 128
 MAXIMG = 256
+
+
+def gather_by_exchange(x, axis, dim):
+    count = lax.axis_size(axis)
+    repeats = [count if d == dim else 1 for d in range(x.ndim)]
+    return lax.all_to_all(jnp.tile(x, repeats), axis, split_axis=dim, concat_axis=dim, tiled=True)
 
 
 def with_halo(cells, sides, width):
@@ -40,7 +46,7 @@
 
 
 def gather_cols(values):
-    return lax.all_gather(values, "col", axis=0, tiled=True)
+    return gather_by_exchange(values, "col", 0)
 
 
 def out_project(attended, weight):

time: 571 us -> 553 us (0.968)
  waiting for transfers between devices: 320 us -> 262 us
  blocking collectives: 21.2 us -> 66.8 us
  matrix products: 69.7 us -> 62 us
    all_gather x2 -> x0, waiting for transfers between devices: 56.8 us -> none  [gather_cols(): return lax.all_gather(values, 'col', axis=0, tiled=True)]
    all_to_all x0 -> x2, blocking collectives: none -> 46 us  [gather_by_exchange(): lax.all_to_all(jnp.tile(x, repeats), axis, split_axis=dim, concat_axis=di...]
    dot_general x6, matrix products: 27.6 us -> 19.9 us  [head_project(): jnp.dot(values, w, preferred_element_type=jnp.float32).astype(jnp.bfloat16)]
  transfers between devices with their start and end apart: 14 -> 12, of which waited for: 13 -> 11; matrix products, arithmetic and copies ran while one was open for 2% -> 2% of each run, Pallas kernels for 0% -> 0%
where the time goes in v1:
time: 553 us; the launch traced here: 545 us
  waiting for transfers between devices  262 us (47%)
  blocking collectives  66.8 us (12%)
  other arithmetic  63.5 us (11%)
  matrix products  62 us (11%)
  local copies, waits for them, and re-layouts  61.6 us (11%)
  starting transfers between devices  15 us (3%)
  between operations  14.1 us (3%)
    all_gather x1, waiting for transfers between devices, per_device(): piece = lax.all_gather(dec_pairs, 'req', axis=1, tiled=True)  83.5 us
    reduce_scatter x2, waiting for transfers between devices, head_project(): return lax.psum_scatter(stacked, 'row', scatter_dimension=0, tiled=True)  65.2 us
    reduce_scatter x2, waiting for transfers between devices, out_project_heads(): lax.psum_scatter(summed.astype(jnp.bfloat16), 'col', scatter_dimension=0,...  49.6 us
    all_to_all x2, blocking collectives, gather_by_exchange(): lax.all_to_all(jnp.tile(x, repeats), axis, split_axis=dim, concat_axis=di...  46 us
    all_gather x2, waiting for transfers between devices, out_project_heads(): whole = lax.all_gather(attended, 'row', axis=0, tiled=False)  44.1 us
    another operation x12, local copies, waits for them, and re-layouts, head_project(): stacked = jnp.stack(parts, axis=2).transpose(1, 0, 2, 3)  36.8 us
    sub x1, other arithmetic, attend_block(): weights = jnp.where(allowed[None], jnp.exp(scores - peak), 0.0)  36.8 us
    dot_general x6, matrix products, head_project(): jnp.dot(values, w, preferred_element_type=jnp.float32).astype(jnp.bfloat16)  19.9 us
  transfers between devices with their start and end apart: 12, of which 11 were waited for; matrix products, arithmetic and copies ran while one was open for 2% of the time, Pallas kernels for 0%

profile of v1, /device:TPU:0, one launch (start us, length us, event | category | flops | bytes accessed | tf_op | source)
XLA Modules:
  0.0 545.4 jit_solution(15849691878108224303)
XLA Ops:
  6.5 1.2 fusion.34
  7.8 7.0 %psum.14 = f32[128]{0:T(128)S(1)} all-reduce(f32[128]{0:T(128)S(1)} %fusion.34), channel_id=1, replica_groups=mesh['req'=8,'row'=4,'col'=4] {'row'}, use_global_device_ids=true, to_apply=%region_3.4 | all-reduce | flops 128 | bytes 1024 | tf_op jit(solution)/shard_map/psum | solution.py:43
  15.6 1.1 fusion.36
  16.8 19.0 %all_to_all.18 = bf16[4,128,1024]{2,1,0:T(8,128)(2,1)S(1)} all-to-all(bf16[4,128,1024]{2,1,0:T(8,128)(2,1)S(1)} %tile.4), channel_id=1, replica_groups=mesh['req'=8,'row'=4,'col'=4] {'col'}, dimensions={0} | all-to-all | bytes 2097152 | tf_op jit(solution)/shard_map/all_to_all | solution.py:14
  35.8 1.0 copy-done.4
  36.8 2.2 convolution_convert_fusion.3
  39.1 1.9 stack_reshape.20
  40.9 2.3 copy.31
  43.3 4.3 convolution_convert_fusion.4
  47.6 2.3 convolution_convert_fusion.5
  49.9 1.9 stack_reshape.18
  51.7 2.4 copy.29
  54.1 1.9 stack_reshape.19
  55.9 2.3 copy.30
  58.3 4.2 pad_maximum_fusion.1
  62.5 2.7 copy.45
  65.8 8.1 %all_gather.14 = s32[2,512]{1,0:T(2,128)S(1)} all-gather(s32[2,128]{1,0:T(2,128)S(1)} %pad_add_fusion.1), channel_id=1, replica_groups=mesh['req'=8,'row'=4,'col'=4] {'col'}, dimensions={1}, use_global_device_ids=true | all-gather | bytes 5120 | tf_op jit(solution)/shard_map/all_gather | solution.py:158
  74.0 4.9 collective-permute-start
  79.0 1.3 collective-permute-start.1
  80.3 5.8 %collective-permute-done.1 = s32[2,255]{1,0:T(2,128)S(1)} collective-permute-done((s32[2,255]{1,0:T(2,128)S(1)}, s32[2,255]{1,0:T(2,128)S(1)}, u32[]{:S(2)}, u32[]{:S(2)}) %collective-permute-start.1) | collective-permute-done | bytes 2072 | tf_op jit(solution)/shard_map/ppermute | solution.py:27
  86.2 15.4 %reduce-scatter.5.cloned.1.call-done = bf16[512,768]{0,1:T(8,128)(2,1)} async-done(((bf16[2048,768]{0,1:T(8,128)(2,1)}), bf16[512,768]{0,1:T(8,128)(2,1)}) %reduce-scatter.5.cloned.1.call-update) | async-done | bytes 786448 | tf_op jit(solution)/shard_map/reduce_scatter | solution.py:124
  101.7 1.2 fusion.67
  103.7 5.3 collective-permute-start.2
  109.0 1.7 collective-permute-start.3
  110.8 2.3 gather_fusion.2
  114.5 7.8 %collective-permute-done.3 = bf16[2,255,256]{1,2,0:T(8,128)(2,1)} collective-permute-done((bf16[2,255,256]{1,2,0:T(8,128)(2,1)}, bf16[2,255,256]{1,2,0:T(8,128)(2,1)}, u32[]{:S(2)}, u32[]{:S(2)}) %collective-permute-start.3) | collective-permute-done | bytes 261152 | tf_op jit(solution)/shard_map/ppermute | solution.py:27
  122.3 1.5 pad_maximum_fusion.2
  124.7 4.6 fusion.70
  129.3 2.4 fusion.25
  132.6 21.4 %all-gather.4.cloned.1.call-done = bf16[4,512,256]{2,1,0:T(8,128)(2,1)} async-done(((bf16[1,512,256]{2,1,0:T(8,128)(2,1)}), bf16[4,512,256]{2,1,0:T(8,128)(2,1)}) %all-gather.4.cloned.1.call-update) | async-done | bytes 1048592 | tf_op jit(solution)/shard_map/all_gather | solution.py:129
  154.0 4.2 bitcast_convert_fusion.1
  158.9 1.4 gather_fusion.1
  160.4 22.6 %reduce-scatter.7.cloned.1.call-done = bf16[128,1024]{1,0:T(8,128)(2,1)} async-done(((bf16[512,1024]{1,0:T(8,128)(2,1)}), bf16[128,1024]{1,0:T(8,128)(2,1)}) %reduce-scatter.7.cloned.1.call-update) | async-done | bytes 262160 | tf_op jit(solution)/shard_map/reduce_scatter | solution.py:132
  183.0 1.0 fusion.37
  184.1 1.3 collective-permute-start.4
  185.4 1.4 gather_fusion
  186.8 5.6 %collective-permute-done.4 = bf16[128,1024]{1,0:T(8,128)(2,1)S(1)} collective-permute-done((bf16[128,1024]{1,0:T(8,128)(2,1)S(1)}, bf16[128,1024]{1,0:T(8,128)(2,1)S(1)}, u32[]{:S(2)}, u32[]{:S(2)}) %collective-permute-start.4) | collective-permute-done | bytes 262176 | tf_op jit(solution)/shard_map/ppermute | solution.py:37
  192.3 1.4 multiply_reduce_fusion
  193.7 5.7 %psum.15 = f32[192]{0:T(256)S(1)} all-reduce(f32[192]{0:T(256)S(1)} %get-tuple-element.23), channel_id=1, replica_groups=mesh['req'=8,'row'=4,'col'=4] {'row'}, use_global_device_ids=true, to_apply=%region_9.10 | all-reduce | flops 192 | bytes 1536 | tf_op jit(solution)/shard_map/psum | solution.py:43
  199.8 27.0 %all_to_all.19 = bf16[4,192,1024]{2,1,0:T(8,128)(2,1)S(1)} all-to-all(bf16[4,192,1024]{2,1,0:T(8,128)(2,1)S(1)} %tile.5), channel_id=1, replica_groups=mesh['req'=8,'row'=4,'col'=4] {'col'}, dimensions={0} | all-to-all | bytes 3145728 | tf_op jit(solution)/shard_map/all_to_all | solution.py:14
  226.8 1.1 copy-done.2
  227.9 3.0 convolution_convert_fusion
  230.9 3.9 stack_reshape.23
  234.8 4.2 copy.37
  239.0 5.2 convolution_convert_fusion.1
  244.2 3.0 convolution_convert_fusion.2
  247.1 3.9 stack_reshape.21
  251.0 4.2 copy.35
  255.2 3.9 stack_reshape.22
  259.1 4.2 copy.36
  263.3 6.0 %pad_maximum_fusion = bf16[768,4,3,256]{0,1,3,2:T(4,128)(2,1)S(1)} fusion(bf16[768,4,1,256]{0,1,3,2:T(4,128)(2,1)} %copy.37, bf16[768,4,1,256]{0,1,3,2:T(4,128)(2,1)} %copy.36, bf16[768,4,1,256]{0,1,3,2:T(4,128)(2,1)} %copy.35), kind=kLoop, calls=%fused_computation.14 | loop fusion | flops 4718592 | bytes 9437184 | tf_op jit(solution)/shard_map/stack | solution.py:122
  269.3 3.2 copy.46
  272.5 49.8 %reduce-scatter.9.cloned.1.call-done = bf16[768,768]{0,1:T(8,128)(2,1)} async-done(((bf16[3072,768]{0,1:T(8,128)(2,1)}), bf16[768,768]{0,1:T(8,128)(2,1)}) %reduce-scatter.9.cloned.1.call-update) | async-done | bytes 1179664 | tf_op jit(solution)/shard_map/reduce_scatter | solution.py:124
  322.3 1.3 fusion.65
  324.8 5.7 %iota_compare_fusion = pred[768,6144]{1,0:T(8,128)(4,1)} fusion(s32[768]{0:T(1024)S(1)} %iota_add_fusion), kind=kLoop, calls=%fused_computation.12 | loop fusion | flops 4718592 | bytes 4721664 | tf_op jit(solution)/shard_map/ge | solution.py:215
  330.5 83.5 %all-gather.6.cloned.1.call-done = bf16[2,6144,256]{1,2,0:T(8,128)(2,1)} async-done(((bf16[2,768,256]{1,2,0:T(8,128)(2,1)}), bf16[2,6144,256]{1,2,0:T(8,128)(2,1)}) %all-gather.6.cloned.1.call-update) | async-done | bytes 6291472 | tf_op jit(solution)/shard_map/all_gather | solution.py:212
  414.0 5.4 fusion.64
  419.4 14.7 %fusion.72 = f32[2,768,6144]{2,1,0:T(8,128)} fusion(bf16[768,2,128]{0,2,1:T(8,128)(2,1)S(1)} %bitcast.98, bf16[6144,2,128]{0,2,1:T(8,128)(2,1)S(1)} %bitcast.92), kind=kOutput, calls=%fused_computation.120 | convolution fusion | flops 2415919104 | bytes 41287680 | tf_op jit(solution)/shard_map/qhd,khd->hqk/dot_general | solution.py:68
  434.2 36.8 %fusion.71 = (f32[2,768]{1,0:T(2,128)S(1)}, bf16[2,768,6144]{2,1,0:T(8,128)(2,1)}) fusion(f32[2,768,6144]{2,1,0:T(8,128)} %fusion.72, pred[768,6144]{1,0:T(8,128)(4,1)S(1)} %bitcast.96), kind=kOutput, calls=%fused_computation.119 | output fusion | flops 75503616 | bytes 61347840 | tf_op jit(solution)/shard_map/sub | solution.py:73
  471.0 10.4 %fusion.31 = bf16[768,2,128]{0,2,1:T(8,128)(2,1)S(1)} fusion(bf16[6144,2,128]{0,2,1:T(8,128)(2,1)} %bitcast.97, bf16[2,768,6144]{2,1,0:T(8,128)(2,1)} %get-tuple-element.26, f32[768,2]{0,1:T(2,128)S(1)} %bitcast.115), kind=kOutput, calls=%fused_computation.41 | convolution fusion | flops 2416312320 | bytes 22419456 | tf_op jit(solution)/shard_map/hqk,khd->qhd/dot_general | solution.py:75
  482.4 22.7 %all-gather.8.cloned.1.call-done = bf16[4,768,256]{2,1,0:T(8,128)(2,1)} async-done(((bf16[1,768,256]{2,1,0:T(8,128)(2,1)}), bf16[4,768,256]{2,1,0:T(8,128)(2,1)}) %all-gather.8.cloned.1.call-update) | async-done | bytes 1572880 | tf_op jit(solution)/shard_map/all_gather | solution.py:129
  505.1 4.4 bitcast_convert_fusion
  509.5 27.0 %reduce-scatter.11.cloned.1.call-done = bf16[192,1024]{1,0:T(8,128)(2,1)} async-done(((bf16[768,1024]{1,0:T(8,128)(2,1)}), bf16[192,1024]{1,0:T(8,128)(2,1)}) %reduce-scatter.11.cloned.1.call-update) | async-done | bytes 393232 | tf_op jit(solution)/shard_map/reduce_scatter | solution.py:132
  536.5 1.8 add_convert_fusion
  (83 shorter events, 9.4 us)
Async XLA Ops:
  6.5 498.5 %copy-start = (bf16[1024,1024]{1,0:T(8,128)(2,1)S(1)}, bf16[1024,1024]{1,0:T(8,128)(2,1)}, u32[]{:S(2)}) copy-start(bf16[1024,1024]{1,0:T(8,128)(2,1)} %param.27) | copy-start | bytes 6291460
  6.5 95.1 %reduce-scatter.5.cloned.1.call-start = ((), (), s32[]{:S(2)}) async-start(), calls=%async_computation.6 | async-start | bytes 3932160 | tf_op jit(solution)/shard_map/reduce_scatter | solution.py:124
  14.7 22.1 %copy-start.9 = (bf16[1024,1024]{1,0:T(8,128)(2,1)S(1)}, bf16[1024,1024]{1,0:T(8,128)(2,1)}, u32[]{:S(2)}) copy-start(bf16[1024,1024]{1,0:T(8,128)(2,1)} %param.21) | copy-start | bytes 6291460
  35.8 1.0 copy-start.4
  43.2 4.3 copy-start.5
  43.3 4.3 copy-start.10
  65.1 0.7 copy-start.7
  65.1 0.7 copy-start.8
  65.2 88.8 %all-gather.4.cloned.1.call-start = ((), (), s32[]{:S(2)}) async-start(), calls=%async_computation.7 | async-start | bytes 1310720 | tf_op jit(solution)/shard_map/all_gather | solution.py:129
  74.0 6.3 %collective-permute-start = (s32[2,255]{1,0:T(2,128)S(1)}, s32[2,255]{1,0:T(2,128)S(1)}, u32[]{:S(2)}, u32[]{:S(2)}) collective-permute-start(s32[2,255]{1,0:T(2,128)S(1)} %get-tuple-element.19), channel_id=1, source_target_pairs={{0,16},{16,32},{32,48},{48,64},{64,80},{80,96},{96,112},{1,17},{17... | collective-permute-start | bytes 6128 | tf_op jit(solution)/shard_map/ppermute | solution.py:25
  79.0 7.2 %collective-permute-start.1 = (s32[2,255]{1,0:T(2,128)S(1)}, s32[2,255]{1,0:T(2,128)S(1)}, u32[]{:S(2)}, u32[]{:S(2)}) collective-permute-start(s32[2,255]{1,0:T(2,128)S(1)} %get-tuple-element.20), channel_id=1, source_target_pairs={{16,0},{32,16},{48,32},{64,48},{80,64},{96,80},{112,96},{17,1},{33... | collective-permute-start | bytes 6128 | tf_op jit(solution)/shard_map/ppermute | solution.py:27
  103.7 10.8 %collective-permute-start.2 = (bf16[2,255,256]{1,2,0:T(8,128)(2,1)}, bf16[2,255,256]{1,2,0:T(8,128)(2,1)}, u32[]{:S(2)}, u32[]{:S(2)}) collective-permute-start(bf16[2,255,256]{1,2,0:T(8,128)(2,1)} %get-tuple-element.15), channel_id=1, source_target_pairs={{0,16},{16,32},{32,48},{48,64},{64,80},{80,96},{96,112},{1,17},{17... | collective-permute-start | bytes 783368 | tf_op jit(solution)/shard_map/ppermute | solution.py:25
  109.0 13.3 %collective-permute-start.3 = (bf16[2,255,256]{1,2,0:T(8,128)(2,1)}, bf16[2,255,256]{1,2,0:T(8,128)(2,1)}, u32[]{:S(2)}, u32[]{:S(2)}) collective-permute-start(bf16[2,255,256]{1,2,0:T(8,128)(2,1)} %get-tuple-element.16), channel_id=1, source_target_pairs={{16,0},{32,16},{48,32},{64,48},{80,64},{96,80},{112,96},{17,1},{33... | collective-permute-start | bytes 783368 | tf_op jit(solution)/shard_map/ppermute | solution.py:27
  132.6 50.5 %reduce-scatter.7.cloned.1.call-start = ((), (), s32[]{:S(2)}) async-start(), calls=%async_computation.8 | async-start | bytes 1310720 | tf_op jit(solution)/shard_map/reduce_scatter | solution.py:132
  154.0 4.2 copy-start.6
  158.1 24.9 %copy-start.1 = (bf16[128,1024]{1,0:T(8,128)(2,1)S(1)}, bf16[128,1024]{1,0:T(8,128)(2,1)}, u32[]{:S(2)}) copy-start(bf16[128,1024]{1,0:T(8,128)(2,1)} %param.15) | copy-start | bytes 786436
  158.2 164.1 %reduce-scatter.9.cloned.1.call-start = ((), (), s32[]{:S(2)}) async-start(), calls=%async_computation.9 | async-start | bytes 5898240 | tf_op jit(solution)/shard_map/reduce_scatter | solution.py:124
  184.1 8.3 %collective-permute-start.4 = (bf16[128,1024]{1,0:T(8,128)(2,1)S(1)}, bf16[128,1024]{1,0:T(8,128)(2,1)S(1)}, u32[]{:S(2)}, u32[]{:S(2)}) collective-permute-start(bf16[128,1024]{1,0:T(8,128)(2,1)S(1)} %fusion.37), channel_id=1, source_target_pairs={{1,0},{2,1},{3,2},{16,3},{17,16},{18,17},{19,18},{32,19},{33,32},{... | collective-permute-start | bytes 786440 | tf_op jit(solution)/shard_map/ppermute | solution.py:37
  199.5 28.4 %copy-start.11 = (bf16[1024,1024]{1,0:T(8,128)(2,1)S(1)}, bf16[1024,1024]{1,0:T(8,128)(2,1)}, u32[]{:S(2)}) copy-start(bf16[1024,1024]{1,0:T(8,128)(2,1)} %param.26) | copy-start | bytes 6291460
  226.8 1.2 copy-start.2
  239.0 5.2 copy-start.3
  239.0 5.2 copy-start.12
  272.5 141.5 %all-gather.6.cloned.1.call-start = ((), (), s32[]{:S(2)}) async-start(), calls=%async_computation.10 | async-start | bytes 7077888 | tf_op jit(solution)/shard_map/all_gather | solution.py:212
  324.5 180.5 %all-gather.8.cloned.1.call-start = ((), (), s32[]{:S(2)}) async-start(), calls=%async_computation.11 | async-start | bytes 1966080 | tf_op jit(solution)/shard_map/all_gather | solution.py:129
  414.0 20.2 %slice-start = ((s8[4718592]{0:T(1024)(128)(4,1)}), s8[4194304]{0:T(1024)(128)(4,1)S(1)}, s32[]{:S(2)}) async-start(s8[4718592]{0:T(1024)(128)(4,1)} %bitcast.95), calls=%async_computation.13 | async-start | bytes 8388608
  419.4 14.7 %slice-start.1 = ((s8[4718592]{0:T(1024)(128)(4,1)}), s8[524288]{0:T(1024)(128)(4,1)S(1)}, s32[]{:S(2)}) async-start(s8[4718592]{0:T(1024)(128)(4,1)} %bitcast.95), calls=%async_computation.14 | async-start | bytes 1048576
  482.3 54.2 %reduce-scatter.11.cloned.1.call-start = ((), (), s32[]{:S(2)}) async-start(), calls=%async_computation.12 | async-start | bytes 1966080 | tf_op jit(solution)/shard_map/reduce_scatter | solution.py:132
Sparse Core Ops, SparseCore 0:
  65.3 36.3 reduce-scatter.4
  132.7 21.2 all-gather.3
  158.3 24.6 reduce-scatter.6
  272.6 49.6 reduce-scatter.8
  324.7 89.2 all-gather.5
  482.4 22.6 all-gather.7
  509.6 26.8 reduce-scatter.10
